TPU v7x, 32 devices: a whole 2x2x4 slice. The times are simulated.
32 devices in a mesh: gx: 4 (over x, core), gy: 8 (over z, y).
Axes of the slice: x: 2, y: 2, z: 4, core: 2. Of those that a mesh axis runs over, the one named last changes fastest.
Arguments:
- right_side: float32 [4, 1024, 2048], P(None, 'gx', 'gy')
- prior_weight: float32 [4, 1024, 2048], P(None, 'gx', 'gy'), may hold values from 0.5 to 4
- jacobi_inverse: float32 [4, 1024, 2048], P(None, 'gx', 'gy'), may hold values from 0.1 to 0.5
- interaction: float32 [2, 4, 128, 128], replicated, may hold values from -0.5 to 0.5
- footprint: int32 [2, 16, 16, 4], P(None, 'gx', 'gy'), may hold values from 0 to 255, as said below
Outputs:
- solution: float32 [4, 1024, 2048], P(None, 'gx', 'gy')
- residual: float32 [4, 1024, 2048], P(None, 'gx', 'gy')
Inputs may be any that keep to these rules, and one draw needn't show every extreme that they name: `footprint`: each entry is bx * 16 + by of a block of the same 4 block rows along the first dimension as its ray block's tile. Of the 64 entries of one tile's ray blocks, between 7 and 9 fall in each tile of the same strip along the second dimension, exactly 9 in some; one tile of the second dimension receives exactly 9 entries from every tile of the strip.
All inputs are finite; a program needn't handle non-finite values.
Results may differ from a plain program's by a relative error of at most 0.0003.
Values sent between devices are 32-bit elements; how exact they have to be, the bound alone decides.
No kernel may reach another device: no remote copies, remote signals or barrier semaphores. Data moves between devices by JAX's collectives and lax.ppermute only.
A program may use at most 128 MiB of HBM per device.

v0:
```python
import jax
import jax.numpy as jnp
from jax import lax
from jax.sharding import PartitionSpec as P

ITERS = 4
DAUB_LOW = (
    0.3326705529509569,
    0.8068915093133388,
    0.4598775021193313,
    -0.13501102001039084,
    -0.08544127388224149,
    0.035226291882100656,
)
DAUB_HIGH = tuple(((-1.0) ** tap_index * DAUB_LOW[5 - tap_index] for tap_index in range(6)))


def extended(block, sides, width):
    for axis, dim in sides:
        count = lax.axis_size(axis)
        forward = [(i, i + 1) for i in range(count - 1)]
        backward = [(target, source) for source, target in forward]
        low = lax.ppermute(
            lax.slice_in_dim(block, block.shape[dim] - width, None, axis=dim), axis, forward
        )
        high = lax.ppermute(lax.slice_in_dim(block, 0, width, axis=dim), axis, backward)
        block = jnp.concatenate([low, block, high], axis=dim)
    return block


def synth_table(length):
    inputs = jnp.arange(length + 8, dtype=jnp.int32)[:, None]
    outputs = jnp.arange(length, dtype=jnp.int32)[None, :]
    half = outputs // 2
    phase = outputs % 2
    table = jnp.zeros((length + 8, length), jnp.float32)
    for tap_num in range(3):
        low_coef = jnp.where(phase == 0, DAUB_LOW[2 * tap_num], DAUB_LOW[2 * tap_num + 1])
        high_coef = jnp.where(phase == 0, DAUB_HIGH[2 * tap_num], DAUB_HIGH[2 * tap_num + 1])
        table = table + jnp.where(inputs == 2 * (half - tap_num) + 4, low_coef, 0.0)
        table = table + jnp.where(inputs == 2 * (half - tap_num) + 5, high_coef, 0.0)
    return table


def analysis_table(length):
    inputs = jnp.arange(length + 8, dtype=jnp.int32)[:, None]
    outputs = jnp.arange(length, dtype=jnp.int32)[None, :]
    half = outputs // 2
    phase = outputs % 2
    table = jnp.zeros((length + 8, length), jnp.float32)
    for tap_num in range(3):
        for offset in (0, 1):
            coef = jnp.where(
                phase == 0, DAUB_LOW[2 * tap_num + offset], DAUB_HIGH[2 * tap_num + offset]
            )
            table = table + jnp.where(inputs == 2 * (half + tap_num) + offset + 4, coef, 0.0)
    return table


def butterfly_sum(value, axis):
    count = lax.axis_size(axis)
    if count & count - 1:
        return lax.psum(value, axis)
    stride = 1
    while stride < count:
        value = value + lax.ppermute(value, axis, [(i, i ^ stride) for i in range(count)])
        stride *= 2
    return value


def global_sum(local_value):
    return butterfly_sum(butterfly_sum(local_value, "gx"), "gy")


def with_rim(field):
    return extended(field, (("gx", 1), ("gy", 2)), 4)


def shards(right_side, prior_weight, jacobi_inverse, interaction, footprint):
    highest = lax.Precision.HIGHEST
    layers, tile_rows, tile_cols = right_side.shape
    sensors, rows_blocks, cols_blocks = (footprint.shape[0], footprint.shape[1], footprint.shape[2])
    block_rows = tile_rows // rows_blocks
    block_cols = tile_cols // cols_blocks
    owners = lax.axis_size("gy")
    layer_blocks_cols = cols_blocks * owners
    requests = sensors * rows_blocks * cols_blocks * layers
    capacity = requests // owners + 1
    own_blocks = layers * rows_blocks * cols_blocks
    synth_rows = synth_table(tile_rows)
    synth_cols = synth_table(tile_cols)
    analysis_rows = analysis_table(tile_rows)
    analysis_cols = analysis_table(tile_cols)
    flat_ids = footprint.reshape(requests)
    request_num = jnp.arange(requests, dtype=jnp.int32)
    layer_of = request_num % layers
    sensor_of = request_num // (requests // sensors)
    target = flat_ids % layer_blocks_cols // cols_blocks
    owned_index = (
        layer_of * (rows_blocks * cols_blocks)
        + flat_ids // layer_blocks_cols % rows_blocks * cols_blocks
        + flat_ids % layer_blocks_cols % cols_blocks
    )
    picks = (target[:, None] == jnp.arange(owners, dtype=jnp.int32)[None, :]).astype(jnp.int32)
    slot = jnp.sum(picks * (jnp.cumsum(picks, axis=0) - 1), axis=1)
    send_ids = jnp.full((owners, capacity), own_blocks, jnp.int32).at[target, slot].set(owned_index)
    send_pairs = (
        jnp.zeros((owners, capacity), jnp.int32).at[target, slot].set(sensor_of * layers + layer_of)
    )
    wanted_ids, wanted_pairs = (
        lax.all_to_all(send_ids, "gy", split_axis=0, concat_axis=0, tiled=True),
        lax.all_to_all(send_pairs, "gy", split_axis=0, concat_axis=0, tiled=True),
    )
    slot_source = (
        jnp.full((owners, capacity), requests, jnp.int32).at[target, slot].set(request_num)
    )
    landing = (
        wanted_ids.reshape(-1)[None, :] == jnp.arange(own_blocks, dtype=jnp.int32)[:, None]
    ).astype(jnp.float32)

    def apply_op(direction):
        synthesize_padded = with_rim(direction)
        along_rows = jnp.einsum("lab,ac->lcb", synthesize_padded, synth_rows, precision=highest)
        blocks = (
            jnp.einsum("lab,bc->lac", along_rows, synth_cols, precision=highest)
            .reshape(layers, rows_blocks, block_rows, cols_blocks, block_cols)
            .transpose(0, 1, 3, 2, 4)
            .reshape(own_blocks, block_rows, block_cols)
        )
        outgoing = jnp.take(blocks, wanted_ids, axis=0, mode="fill", fill_value=0.0)
        arrived = lax.all_to_all(outgoing, "gy", split_axis=0, concat_axis=0, tiled=True)
        seen = arrived[target, slot].reshape(
            sensors, rows_blocks * cols_blocks, layers, block_rows, block_cols
        )
        slopes = jnp.einsum("sklxy,slyz->skxz", seen, interaction, precision=highest)
        back = jnp.einsum("skxz,slyz->sklxy", slopes, interaction, precision=highest).reshape(
            requests, block_rows, block_cols
        )
        returning = jnp.take(back, slot_source, axis=0, mode="fill", fill_value=0.0)
        landed = lax.all_to_all(returning, "gy", split_axis=0, concat_axis=0, tiled=True)
        summed = jnp.dot(
            landing, landed.reshape(owners * capacity, block_rows * block_cols), precision=highest
        )
        padded = with_rim(
            summed.reshape(layers, rows_blocks, cols_blocks, block_rows, block_cols)
            .transpose(0, 1, 3, 2, 4)
            .reshape(layers, tile_rows, tile_cols)
        )
        along_cols = jnp.einsum("lab,bc->lac", padded, analysis_cols, precision=highest)
        return (
            jnp.einsum("lab,ac->lcb", along_cols, analysis_rows, precision=highest)
            + prior_weight * direction
        )

    solution = jnp.zeros_like(right_side)
    residual = right_side
    precond_res = jacobi_inverse * residual
    direction = precond_res
    rho_now = global_sum(jnp.sum(residual * precond_res))
    image = apply_op(direction)
    for step in range(ITERS):
        step_size = rho_now / global_sum(jnp.sum(direction * image))
        solution = solution + step_size * direction
        residual = residual - step_size * image
        if step + 1 < ITERS:
            precond_res = jacobi_inverse * residual
            rho_next = global_sum(jnp.sum(residual * precond_res))
            applied = apply_op(precond_res)
            ratio = rho_next / rho_now
            direction = precond_res + ratio * direction
            image = applied + ratio * image
            rho_now = rho_next
    return (solution, residual)


def solution(mesh):
    return jax.shard_map(
        shards,
        mesh=mesh,
        in_specs=(
            P(None, "gx", "gy"),
            P(None, "gx", "gy"),
            P(None, "gx", "gy"),
            P(),
            P(None, "gx", "gy", None),
        ),
        out_specs=(P(None, "gx", "gy"), P(None, "gx", "gy")),
        check_vma=False,
    )
```

profile of v0, /device:TPU:0, one launch (start us, length us, event | category | flops | bytes accessed | tf_op | source)
XLA Modules:
  0.0 1004.9 jit_solution(15432480952967989075)
XLA Ops:
  3.4 10.1 %scatter_fusion = s32[8,9]{1,0:T(8,128)} fusion(s32[8,9]{1,0:T(8,128)} %broadcast_in_dim.425, s32[64]{0:T(128)S(1)} %fusion.183, s32[64]{0:T(128)S(1)} %get-tuple-element.21), kind=kCustom, calls=%fused_computation.12 | custom fusion | bytes 1280 | tf_op jit(solution)/shard_map/scatter | solution.py:106
  13.5 7.3 all-to-all-start
  33.4 3.9 collective-permute-start.7
  38.9 4.2 collective-permute-done.8
  56.5 6.0 all-to-all-start.1
  66.1 48.2 %all-to-all-done.1 = f32[8,9,64,128]{3,2,1,0:T(8,128)} async-done(((f32[8,9,64,128]{3,2,1,0:T(8,128)}), f32[8,9,64,128]{3,2,1,0:T(8,128)}, u32[]{:S(2)}, u32[]{:S(2)}) %all-to-all-start.1) | async-done | bytes 2359328 | tf_op jit(solution)/shard_map/all_to_all | solution.py:131
  131.6 7.1 all-to-all-start.2
  139.9 54.4 %all-to-all-done.2 = f32[8,9,64,128]{3,2,1,0:T(8,128)} async-done(((f32[8,9,64,128]{3,2,1,0:T(8,128)}), f32[8,9,64,128]{3,2,1,0:T(8,128)}, u32[]{:S(2)}, u32[]{:S(2)}) %all-to-all-start.2) | async-done | bytes 2359328 | tf_op jit(solution)/shard_map/all_to_all | solution.py:140
  213.5 4.5 collective-permute-start.11
  221.0 3.8 fusion.18
  224.8 4.5 multiply_reduce_fusion.6
  245.7 4.1 collective-permute-start.16
  254.6 4.0 collective-permute-start.4
  266.6 4.1 collective-permute-done.24
  275.0 4.9 collective-permute-done.26
  282.3 3.8 fusion.199
  296.3 59.0 %all_to_all.52 = f32[8,9,64,128]{3,2,1,0:T(8,128)} all-to-all(f32[8,9,64,128]{3,2,1,0:T(8,128)S(1)} %broadcast_select_fusion.5), channel_id=1, replica_groups=mesh['gx'=4,'gy'=8] {'gy'}, dimensions={0} | all-to-all | bytes 4718592 | tf_op jit(solution)/shard_map/all_to_all | solution.py:131
  371.3 59.9 %all_to_all.53 = f32[8,9,64,128]{3,2,1,0:T(8,128)S(1)} all-to-all(f32[8,9,64,128]{3,2,1,0:T(8,128)S(1)} %broadcast_select_fusion.4), channel_id=1, replica_groups=mesh['gx'=4,'gy'=8] {'gy'}, dimensions={0} | all-to-all | bytes 4718592 | tf_op jit(solution)/shard_map/all_to_all | solution.py:140
  479.4 3.8 fusion.38
  483.2 4.6 multiply_reduce_fusion.4
  523.4 4.2 collective-permute-done.44
  530.0 3.8 fusion.196
  544.0 56.9 %all_to_all.54 = f32[8,9,64,128]{3,2,1,0:T(8,128)} all-to-all(f32[8,9,64,128]{3,2,1,0:T(8,128)S(1)} %broadcast_select_fusion.3), channel_id=1, replica_groups=mesh['gx'=4,'gy'=8] {'gy'}, dimensions={0} | all-to-all | bytes 4718592 | tf_op jit(solution)/shard_map/all_to_all | solution.py:131
  616.8 59.8 %all_to_all.55 = f32[8,9,64,128]{3,2,1,0:T(8,128)S(1)} all-to-all(f32[8,9,64,128]{3,2,1,0:T(8,128)S(1)} %broadcast_select_fusion.2), channel_id=1, replica_groups=mesh['gx'=4,'gy'=8] {'gy'}, dimensions={0} | all-to-all | bytes 4718592 | tf_op jit(solution)/shard_map/all_to_all | solution.py:140
  724.5 3.9 fusion.58
  728.4 5.2 multiply_reduce_fusion.2
  769.4 3.9 collective-permute-done.62
  775.7 3.8 fusion.193
  789.7 56.9 %all_to_all.56 = f32[8,9,64,128]{3,2,1,0:T(8,128)} all-to-all(f32[8,9,64,128]{3,2,1,0:T(8,128)S(1)} %broadcast_select_fusion.1), channel_id=1, replica_groups=mesh['gx'=4,'gy'=8] {'gy'}, dimensions={0} | all-to-all | bytes 4718592 | tf_op jit(solution)/shard_map/all_to_all | solution.py:131
  862.6 59.7 %all_to_all.57 = f32[8,9,64,128]{3,2,1,0:T(8,128)S(1)} all-to-all(f32[8,9,64,128]{3,2,1,0:T(8,128)S(1)} %broadcast_select_fusion), channel_id=1, replica_groups=mesh['gx'=4,'gy'=8] {'gy'}, dimensions={0} | all-to-all | bytes 4718592 | tf_op jit(solution)/shard_map/all_to_all | solution.py:140
  970.1 3.9 fusion.78
  974.0 4.6 multiply_reduce_fusion
  (319 shorter events, 404.5 us)
Async XLA Ops:
  13.5 15.8 %all-to-all-start = ((s32[8,1,9]{2,1,0:T(1,128)}), s32[8,1,9]{2,1,0:T(1,128)S(1)}, u32[]{:S(2)}, u32[]{:S(2)}) async-start(s32[8,1,9]{2,1,0:T(1,128)} %bitcast.4), calls=%async_computation | async-start | bytes 8192 | tf_op jit(solution)/shard_map/all_to_all | solution.py:111
  28.0 5.3 collective-permute-start.6
  33.4 5.4 collective-permute-start.7
  37.4 5.7 collective-permute-start.8
  56.5 57.7 %all-to-all-start.1 = ((f32[8,9,64,128]{3,2,1,0:T(8,128)}), f32[8,9,64,128]{3,2,1,0:T(8,128)}, u32[]{:S(2)}, u32[]{:S(2)}) async-start(f32[8,9,64,128]{3,2,1,0:T(8,128)} %broadcast_select_fusion.7), calls=%async_computation.1 | async-start | bytes 4718592 | tf_op jit(solution)/shard_map/all_to_all | solution.py:131
  131.6 62.8 %all-to-all-start.2 = ((f32[8,9,64,128]{3,2,1,0:T(8,128)}), f32[8,9,64,128]{3,2,1,0:T(8,128)}, u32[]{:S(2)}, u32[]{:S(2)}) async-start(f32[8,9,64,128]{3,2,1,0:T(8,128)} %broadcast_select_fusion.6), calls=%async_computation.2 | async-start | bytes 4718592 | tf_op jit(solution)/shard_map/all_to_all | solution.py:140
  212.2 7.7 collective-permute-start.12
  213.5 6.1 collective-permute-start.11
  233.1 5.9 collective-permute-start.14
  236.4 6.6 collective-permute-start.1
  239.8 5.4 collective-permute-start.15
  243.7 6.1 collective-permute-start.2
  245.7 6.1 collective-permute-start.16
  252.3 6.3 collective-permute-start.17
  254.6 4.6 collective-permute-start.4
  265.1 5.6 collective-permute-start.24
  273.5 6.5 collective-permute-start.26
  450.0 28.0 %collective-permute-start.29 = (f32[4,264,4]{1,2,0:T(4,128)S(1)}, f32[4,264,4]{1,2,0:T(4,128)S(1)}, u32[]{:S(2)}, u32[]{:S(2)}) collective-permute-start(f32[4,264,4]{1,2,0:T(4,128)S(1)} %copy.37), channel_id=1, source_target_pairs={{0,1},{1,2},{2,3},{3,4},{4,5},{5,6},{6,7},{8,9},{9,10},{10,11},{11... | collective-permute-start | bytes 50696 | tf_op jit(solution)/shard_map/ppermute | solution.py:23
  453.6 24.7 %collective-permute-start.30 = (f32[4,264,4]{1,2,0:T(4,128)S(1)}, f32[4,264,4]{1,2,0:T(4,128)S(1)}, u32[]{:S(2)}, u32[]{:S(2)}) collective-permute-start(f32[4,264,4]{1,2,0:T(4,128)S(1)} %copy.38), channel_id=1, source_target_pairs={{1,0},{2,1},{3,2},{4,3},{5,4},{6,5},{7,6},{9,8},{10,9},{11,10},{12... | collective-permute-start | bytes 50696 | tf_op jit(solution)/shard_map/ppermute | solution.py:26
  472.8 4.6 collective-permute-start.22
  513.2 4.8 collective-permute-start.42
  518.1 5.2 collective-permute-start.43
  521.9 5.7 collective-permute-start.44
  695.4 27.7 %collective-permute-start.47 = (f32[4,264,4]{1,2,0:T(4,128)S(1)}, f32[4,264,4]{1,2,0:T(4,128)S(1)}, u32[]{:S(2)}, u32[]{:S(2)}) collective-permute-start(f32[4,264,4]{1,2,0:T(4,128)S(1)} %copy.47), channel_id=1, source_target_pairs={{0,1},{1,2},{2,3},{3,4},{4,5},{5,6},{6,7},{8,9},{9,10},{10,11},{11... | collective-permute-start | bytes 50696 | tf_op jit(solution)/shard_map/ppermute | solution.py:23
  699.0 24.4 %collective-permute-start.48 = (f32[4,264,4]{1,2,0:T(4,128)S(1)}, f32[4,264,4]{1,2,0:T(4,128)S(1)}, u32[]{:S(2)}, u32[]{:S(2)}) collective-permute-start(f32[4,264,4]{1,2,0:T(4,128)S(1)} %copy.48), channel_id=1, source_target_pairs={{1,0},{2,1},{3,2},{4,3},{5,4},{6,5},{7,6},{9,8},{10,9},{11,10},{12... | collective-permute-start | bytes 50696 | tf_op jit(solution)/shard_map/ppermute | solution.py:26
  717.9 4.6 collective-permute-start.40
  759.0 4.8 collective-permute-start.60
  763.9 5.5 collective-permute-start.61
  767.6 5.7 collective-permute-start.62
  941.1 27.7 %collective-permute-start.65 = (f32[4,264,4]{1,2,0:T(4,128)S(1)}, f32[4,264,4]{1,2,0:T(4,128)S(1)}, u32[]{:S(2)}, u32[]{:S(2)}) collective-permute-start(f32[4,264,4]{1,2,0:T(4,128)S(1)} %copy.57), channel_id=1, source_target_pairs={{0,1},{1,2},{2,3},{3,4},{4,5},{5,6},{6,7},{8,9},{9,10},{10,11},{11... | collective-permute-start | bytes 50696 | tf_op jit(solution)/shard_map/ppermute | solution.py:23
  944.7 24.3 %collective-permute-start.66 = (f32[4,264,4]{1,2,0:T(4,128)S(1)}, f32[4,264,4]{1,2,0:T(4,128)S(1)}, u32[]{:S(2)}, u32[]{:S(2)}) collective-permute-start(f32[4,264,4]{1,2,0:T(4,128)S(1)} %copy.58), channel_id=1, source_target_pairs={{1,0},{2,1},{3,2},{4,3},{5,4},{6,5},{7,6},{9,8},{10,9},{11,10},{12... | collective-permute-start | bytes 50696 | tf_op jit(solution)/shard_map/ppermute | solution.py:26
  963.6 4.6 collective-permute-start.58
  (63 other events, 375.8 us)
where the time goes:
time: 1020 us; the launch traced here: 1000 us
  blocking collectives  352 us (35%)
  starting transfers between devices  187 us (18%)
  waiting for transfers between devices  169 us (17%)
  local copies, waits for them, and re-layouts  130 us (13%)
  matrix products  95 us (9%)
  other arithmetic  39.3 us (4%)
  between operations  31.5 us (3%)
    all_to_all x3, blocking collectives, apply_op(): lax.all_to_all(returning, 'gy', split_axis=0, concat_axis=0, tiled=True)  179 us
    all_to_all x3, blocking collectives, apply_op(): lax.all_to_all(outgoing, 'gy', split_axis=0, concat_axis=0, tiled=True)  173 us
    ppermute x40, starting transfers between devices, butterfly_sum(): lax.ppermute(value, axis, [(i, i ^ stride) for i in range(count)])  102 us
    all_to_all x1, waiting for transfers between devices, apply_op(): lax.all_to_all(returning, 'gy', split_axis=0, concat_axis=0, tiled=True)  54.4 us
    all_to_all x1, waiting for transfers between devices, apply_op(): lax.all_to_all(outgoing, 'gy', split_axis=0, concat_axis=0, tiled=True)  48.2 us
    ppermute x16, starting transfers between devices, extended(): lax.ppermute(lax.slice_in_dim(block, block.shape[dim] - width, None, axis...  42.1 us
    ppermute x16, waiting for transfers between devices, extended(): lax.ppermute(lax.slice_in_dim(block, 0, width, axis=dim), axis, backward)  38.6 us
    ppermute x40, waiting for transfers between devices, butterfly_sum(): lax.ppermute(value, axis, [(i, i ^ stride) for i in range(count)])  26.9 us
  transfers between devices with their start and end apart: 75, of which 50 were waited for; matrix products, arithmetic and copies ran while one was open for 1% of the time, Pallas kernels for 0%

commit v1 on v0

--- a/solution.py
+++ b/solution.py
@@ -13,6 +13,29 @@
     0.035226291882100656,
 )
 DAUB_HIGH = tuple(((-1.0) ** tap_index * DAUB_LOW[5 - tap_index] for tap_index in range(6)))
+
+
+def split_up(shard, dim, count):
+    before, after = (shard.shape[:dim], shard.shape[dim + 1 :])
+    return jnp.moveaxis(shard.reshape(*before, count, -1, *after), dim, 0)
+
+
+def in_order(blocks, dim):
+    lengths = list(blocks.shape[1:])
+    lengths[dim] *= blocks.shape[0]
+    return jnp.moveaxis(blocks, 0, dim).reshape(lengths)
+
+
+def sent_to_each(array, axis, split_dim, concat_dim):
+    peers, place = (lax.axis_size(axis), lax.axis_index(axis))
+    blocks = split_up(array, split_dim, peers)
+    out = blocks
+    for step in range(1, peers):
+        target, source = ((place + step) % peers, (place - step) % peers)
+        sent = lax.dynamic_index_in_dim(blocks, target, 0)
+        other = lax.ppermute(sent, axis, [(i, (i + step) % peers) for i in range(peers)])
+        out = lax.dynamic_update_slice_in_dim(out, other, source, axis=0)
+    return in_order(out, concat_dim)
 
 
 def extended(block, sides, width):
@@ -128,7 +151,7 @@
             .reshape(own_blocks, block_rows, block_cols)
         )
         outgoing = jnp.take(blocks, wanted_ids, axis=0, mode="fill", fill_value=0.0)
-        arrived = lax.all_to_all(outgoing, "gy", split_axis=0, concat_axis=0, tiled=True)
+        arrived = sent_to_each(outgoing, "gy", 0, 0)
         seen = arrived[target, slot].reshape(
             sensors, rows_blocks * cols_blocks, layers, block_rows, block_cols
         )

time: 1020 us -> 1060 us (1.039)
  blocking collectives: 352 us -> 171 us
  waiting for transfers between devices: 169 us -> 327 us
  local copies, waits for them, and re-layouts: 130 us -> 163 us
  starting transfers between devices: 187 us -> 217 us
    ppermute x0 -> x28, waiting for transfers between devices: none -> 211 us  [sent_to_each(): lax.ppermute(sent, axis, [(i, (i + step) % peers) for i in range(peers)])]
    all_to_all x3 -> x0, blocking collectives: 173 us -> none  [apply_op(): lax.all_to_all(outgoing, 'gy', split_axis=0, concat_axis=0, tiled=True)]
    all_to_all x1 -> x0, waiting for transfers between devices: 48.2 us -> none  [apply_op(): lax.all_to_all(outgoing, 'gy', split_axis=0, concat_axis=0, tiled=True)]
    ppermute x0 -> x28, starting transfers between devices: none -> 39.3 us  [sent_to_each(): lax.ppermute(sent, axis, [(i, (i + step) % peers) for i in range(peers)])]
    dynamic_update_slice x0 -> x24, local copies, waits for them, and re-layouts: none -> 18.5 us  [sent_to_each(): out = lax.dynamic_update_slice_in_dim(out, other, source, axis=0)]
    dynamic_slice x0 -> x8, local copies, waits for them, and re-layouts: none -> 12.2 us  [sent_to_each(): sent = lax.dynamic_index_in_dim(blocks, target, 0)]
  transfers between devices with their start and end apart: 75 -> 102, of which waited for: 50 -> 66; matrix products, arithmetic and copies ran while one was open for 1% -> 3% of each run, Pallas kernels for 0% -> 0%
where the time goes in v1:
time: 1060 us; the launch traced here: 1050 us
  waiting for transfers between devices  327 us (31%)
  starting transfers between devices  217 us (20%)
  blocking collectives  171 us (16%)
  local copies, waits for them, and re-layouts  163 us (15%)
  matrix products  95.2 us (9%)
  other arithmetic  42.5 us (4%)
  between operations  32.2 us (3%)
    ppermute x28, waiting for transfers between devices, sent_to_each(): lax.ppermute(sent, axis, [(i, (i + step) % peers) for i in range(peers)])  211 us
    all_to_all x3, blocking collectives, apply_op(): lax.all_to_all(returning, 'gy', split_axis=0, concat_axis=0, tiled=True)  171 us
    ppermute x40, starting transfers between devices, butterfly_sum(): lax.ppermute(value, axis, [(i, i ^ stride) for i in range(count)])  105 us
    all_to_all x1, waiting for transfers between devices, apply_op(): lax.all_to_all(returning, 'gy', split_axis=0, concat_axis=0, tiled=True)  53 us
    ppermute x16, starting transfers between devices, extended(): lax.ppermute(lax.slice_in_dim(block, block.shape[dim] - width, None, axis...  39.8 us
    ppermute x28, starting transfers between devices, sent_to_each(): lax.ppermute(sent, axis, [(i, (i + step) % peers) for i in range(peers)])  39.3 us
    ppermute x16, waiting for transfers between devices, extended(): lax.ppermute(lax.slice_in_dim(block, 0, width, axis=dim), axis, backward)  38.5 us
    ppermute x40, waiting for transfers between devices, butterfly_sum(): lax.ppermute(value, axis, [(i, i ^ stride) for i in range(count)])  23.2 us
  transfers between devices with their start and end apart: 102, of which 66 were waited for; matrix products, arithmetic and copies ran while one was open for 3% of the time, Pallas kernels for 0%

profile of v1, /device:TPU:0, one launch (start us, length us, event | category | flops | bytes accessed | tf_op | source)
XLA Modules:
  0.0 1048.3 jit_solution(16029078282045136982)
XLA Ops:
  3.4 10.2 scatter_fusion
  13.6 7.3 all-to-all-start
  38.6 4.2 collective-permute-done.8
  78.1 13.7 %collective-permute-done.11 = f32[1,1,9,64,128]{4,3,2,1,0:T(8,128)} collective-permute-done((f32[1,1,9,64,128]{4,3,2,1,0:T(8,128)S(1)}, f32[1,1,9,64,128]{4,3,2,1,0:T(8,128)}, u32[]{:S(2)}, u32[]{:S(2)}) %collective-permute-start.11) | collective-permute-done | bytes 294944 | tf_op jit(solution)/shard_map/ppermute | solution.py:36
  93.5 30.7 %collective-permute-done.12 = f32[1,1,9,64,128]{4,3,2,1,0:T(8,128)S(1)} collective-permute-done((f32[1,1,9,64,128]{4,3,2,1,0:T(8,128)S(1)}, f32[1,1,9,64,128]{4,3,2,1,0:T(8,128)S(1)}, u32[]{:S(2)}, u32[]{:S(2)}) %collective-permute-start.12) | collective-permute-done | bytes 294944 | tf_op jit(solution)/shard_map/ppermute | solution.py:36
  144.5 4.4 all-to-all-start.1
  150.3 53.0 %all-to-all-done.1 = f32[8,9,64,128]{3,2,1,0:T(8,128)} async-done(((f32[8,9,64,128]{3,2,1,0:T(8,128)}), f32[8,9,64,128]{3,2,1,0:T(8,128)}, u32[]{:S(2)}, u32[]{:S(2)}) %all-to-all-start.1) | async-done | bytes 2359328 | tf_op jit(solution)/shard_map/all_to_all | solution.py:163
  221.7 5.0 collective-permute-start.18
  233.4 4.6 multiply_reduce_fusion.6
  284.4 4.6 collective-permute-done.33
  310.8 6.5 collective-permute-done.34
  329.0 14.5 %collective-permute-done.36 = f32[1,1,9,64,128]{4,3,2,1,0:T(8,128)S(1)} collective-permute-done((f32[1,1,9,64,128]{4,3,2,1,0:T(8,128)S(1)}, f32[1,1,9,64,128]{4,3,2,1,0:T(8,128)S(1)}, u32[]{:S(2)}, u32[]{:S(2)}) %collective-permute-start.36) | collective-permute-done | bytes 294944 | tf_op jit(solution)/shard_map/ppermute | solution.py:36
  344.2 31.3 %collective-permute-done.37 = f32[1,1,9,64,128]{4,3,2,1,0:T(8,128)S(1)} collective-permute-done((f32[1,1,9,64,128]{4,3,2,1,0:T(8,128)S(1)}, f32[1,1,9,64,128]{4,3,2,1,0:T(8,128)S(1)}, u32[]{:S(2)}, u32[]{:S(2)}) %collective-permute-start.37) | collective-permute-done | bytes 294944 | tf_op jit(solution)/shard_map/ppermute | solution.py:36
  394.3 57.2 %all_to_all.32 = f32[8,9,64,128]{3,2,1,0:T(8,128)S(1)} all-to-all(f32[8,9,64,128]{3,2,1,0:T(8,128)S(1)} %broadcast_select_fusion.4), channel_id=1, replica_groups=mesh['gx'=4,'gy'=8] {'gy'}, dimensions={0} | all-to-all | bytes 4718592 | tf_op jit(solution)/shard_map/all_to_all | solution.py:163
  491.3 4.3 collective-permute-start.29
  501.7 4.6 multiply_reduce_fusion.4
  521.4 4.3 collective-permute-start.49
  541.8 4.2 collective-permute-done.58
  567.5 6.9 collective-permute-done.59
  586.4 13.8 %collective-permute-done.61 = f32[1,1,9,64,128]{4,3,2,1,0:T(8,128)S(1)} collective-permute-done((f32[1,1,9,64,128]{4,3,2,1,0:T(8,128)S(1)}, f32[1,1,9,64,128]{4,3,2,1,0:T(8,128)S(1)}, u32[]{:S(2)}, u32[]{:S(2)}) %collective-permute-start.61) | collective-permute-done | bytes 294944 | tf_op jit(solution)/shard_map/ppermute | solution.py:36
  600.9 31.6 %collective-permute-done.62 = f32[1,1,9,64,128]{4,3,2,1,0:T(8,128)S(1)} collective-permute-done((f32[1,1,9,64,128]{4,3,2,1,0:T(8,128)S(1)}, f32[1,1,9,64,128]{4,3,2,1,0:T(8,128)S(1)}, u32[]{:S(2)}, u32[]{:S(2)}) %collective-permute-start.62) | collective-permute-done | bytes 294944 | tf_op jit(solution)/shard_map/ppermute | solution.py:36
  651.4 57.2 %all_to_all.33 = f32[8,9,64,128]{3,2,1,0:T(8,128)S(1)} all-to-all(f32[8,9,64,128]{3,2,1,0:T(8,128)S(1)} %broadcast_select_fusion.2), channel_id=1, replica_groups=mesh['gx'=4,'gy'=8] {'gy'}, dimensions={0} | all-to-all | bytes 4718592 | tf_op jit(solution)/shard_map/all_to_all | solution.py:163
  748.7 4.3 collective-permute-start.54
  759.2 5.2 multiply_reduce_fusion.2
  779.4 4.3 collective-permute-start.74
  825.6 6.9 collective-permute-done.84
  844.5 13.8 %collective-permute-done.86 = f32[1,1,9,64,128]{4,3,2,1,0:T(8,128)S(1)} collective-permute-done((f32[1,1,9,64,128]{4,3,2,1,0:T(8,128)S(1)}, f32[1,1,9,64,128]{4,3,2,1,0:T(8,128)S(1)}, u32[]{:S(2)}, u32[]{:S(2)}) %collective-permute-start.86) | collective-permute-done | bytes 294944 | tf_op jit(solution)/shard_map/ppermute | solution.py:36
  859.0 31.6 %collective-permute-done.87 = f32[1,1,9,64,128]{4,3,2,1,0:T(8,128)S(1)} collective-permute-done((f32[1,1,9,64,128]{4,3,2,1,0:T(8,128)S(1)}, f32[1,1,9,64,128]{4,3,2,1,0:T(8,128)S(1)}, u32[]{:S(2)}, u32[]{:S(2)}) %collective-permute-start.87) | collective-permute-done | bytes 294944 | tf_op jit(solution)/shard_map/ppermute | solution.py:36
  909.5 57.0 %all_to_all.34 = f32[8,9,64,128]{3,2,1,0:T(8,128)S(1)} all-to-all(f32[8,9,64,128]{3,2,1,0:T(8,128)S(1)} %broadcast_select_fusion), channel_id=1, replica_groups=mesh['gx'=4,'gy'=8] {'gy'}, dimensions={0} | all-to-all | bytes 4718592 | tf_op jit(solution)/shard_map/all_to_all | solution.py:163
  1006.8 4.3 collective-permute-start.79
  1017.3 4.5 multiply_reduce_fusion
  1036.8 4.3 collective-permute-start.99
  (434 shorter events, 506.0 us)
Async XLA Ops:
  13.6 15.6 %all-to-all-start = ((s32[8,1,9]{2,1,0:T(1,128)}), s32[8,1,9]{2,1,0:T(1,128)S(1)}, u32[]{:S(2)}, u32[]{:S(2)}) async-start(s32[8,1,9]{2,1,0:T(1,128)} %bitcast.4), calls=%async_computation | async-start | bytes 8192 | tf_op jit(solution)/shard_map/all_to_all | solution.py:134
  56.3 9.5 collective-permute-start.9
  68.2 23.6 %collective-permute-start.11 = (f32[1,1,9,64,128]{4,3,2,1,0:T(8,128)S(1)}, f32[1,1,9,64,128]{4,3,2,1,0:T(8,128)}, u32[]{:S(2)}, u32[]{:S(2)}) collective-permute-start(f32[1,1,9,64,128]{4,3,2,1,0:T(8,128)S(1)} %get-tuple-element.49), channel_id=1, source_target_pairs={{0,3},{1,4},{2,5},{3,6},{4,7},{5,0},{6,1},{7,2},{8,11},{9,12},{10,... | collective-permute-start | bytes 884744 | tf_op jit(solution)/shard_map/ppermute | solution.py:36
  70.4 56.1 %collective-permute-start.15 = (f32[1,1,9,64,128]{4,3,2,1,0:T(8,128)S(1)}, f32[1,1,9,64,128]{4,3,2,1,0:T(8,128)S(1)}, u32[]{:S(2)}, u32[]{:S(2)}) collective-permute-start(f32[1,1,9,64,128]{4,3,2,1,0:T(8,128)S(1)} %get-tuple-element.45), channel_id=1, source_target_pairs={{0,7},{1,0},{2,1},{3,2},{4,3},{5,4},{6,5},{7,6},{8,15},{9,8},{10,9... | collective-permute-start | bytes 884744 | tf_op jit(solution)/shard_map/ppermute | solution.py:36
  72.8 52.9 %collective-permute-start.14 = (f32[1,1,9,64,128]{4,3,2,1,0:T(8,128)S(1)}, f32[1,1,9,64,128]{4,3,2,1,0:T(8,128)S(1)}, u32[]{:S(2)}, u32[]{:S(2)}) collective-permute-start(f32[1,1,9,64,128]{4,3,2,1,0:T(8,128)S(1)} %get-tuple-element.46), channel_id=1, source_target_pairs={{0,6},{1,7},{2,0},{3,1},{4,2},{5,3},{6,4},{7,5},{8,14},{9,15},{10,... | collective-permute-start | bytes 884744 | tf_op jit(solution)/shard_map/ppermute | solution.py:36
  73.7 51.2 %collective-permute-start.13 = (f32[1,1,9,64,128]{4,3,2,1,0:T(8,128)S(1)}, f32[1,1,9,64,128]{4,3,2,1,0:T(8,128)S(1)}, u32[]{:S(2)}, u32[]{:S(2)}) collective-permute-start(f32[1,1,9,64,128]{4,3,2,1,0:T(8,128)S(1)} %get-tuple-element.47), channel_id=1, source_target_pairs={{0,5},{1,6},{2,7},{3,0},{4,1},{5,2},{6,3},{7,4},{8,13},{9,14},{10,... | collective-permute-start | bytes 884744 | tf_op jit(solution)/shard_map/ppermute | solution.py:36
  77.0 47.2 %collective-permute-start.12 = (f32[1,1,9,64,128]{4,3,2,1,0:T(8,128)S(1)}, f32[1,1,9,64,128]{4,3,2,1,0:T(8,128)S(1)}, u32[]{:S(2)}, u32[]{:S(2)}) collective-permute-start(f32[1,1,9,64,128]{4,3,2,1,0:T(8,128)S(1)} %get-tuple-element.48), channel_id=1, source_target_pairs={{0,4},{1,5},{2,6},{3,7},{4,0},{5,1},{6,2},{7,3},{8,12},{9,13},{10,... | collective-permute-start | bytes 884744 | tf_op jit(solution)/shard_map/ppermute | solution.py:36
  144.5 58.8 %all-to-all-start.1 = ((f32[8,9,64,128]{3,2,1,0:T(8,128)}), f32[8,9,64,128]{3,2,1,0:T(8,128)}, u32[]{:S(2)}, u32[]{:S(2)}) async-start(f32[8,9,64,128]{3,2,1,0:T(8,128)} %broadcast_select_fusion.6), calls=%async_computation.1 | async-start | bytes 4718592 | tf_op jit(solution)/shard_map/all_to_all | solution.py:163
  307.9 9.5 collective-permute-start.34
  319.6 23.9 %collective-permute-start.36 = (f32[1,1,9,64,128]{4,3,2,1,0:T(8,128)S(1)}, f32[1,1,9,64,128]{4,3,2,1,0:T(8,128)S(1)}, u32[]{:S(2)}, u32[]{:S(2)}) collective-permute-start(f32[1,1,9,64,128]{4,3,2,1,0:T(8,128)S(1)} %get-tuple-element.42), channel_id=1, source_target_pairs={{0,3},{1,4},{2,5},{3,6},{4,7},{5,0},{6,1},{7,2},{8,11},{9,12},{10,... | collective-permute-start | bytes 884744 | tf_op jit(solution)/shard_map/ppermute | solution.py:36
  322.1 55.6 %collective-permute-start.40 = (f32[1,1,9,64,128]{4,3,2,1,0:T(8,128)S(1)}, f32[1,1,9,64,128]{4,3,2,1,0:T(8,128)S(1)}, u32[]{:S(2)}, u32[]{:S(2)}) collective-permute-start(f32[1,1,9,64,128]{4,3,2,1,0:T(8,128)S(1)} %get-tuple-element.38), channel_id=1, source_target_pairs={{0,7},{1,0},{2,1},{3,2},{4,3},{5,4},{6,5},{7,6},{8,15},{9,8},{10,9... | collective-permute-start | bytes 884744 | tf_op jit(solution)/shard_map/ppermute | solution.py:36
  323.9 53.1 %collective-permute-start.39 = (f32[1,1,9,64,128]{4,3,2,1,0:T(8,128)S(1)}, f32[1,1,9,64,128]{4,3,2,1,0:T(8,128)S(1)}, u32[]{:S(2)}, u32[]{:S(2)}) collective-permute-start(f32[1,1,9,64,128]{4,3,2,1,0:T(8,128)S(1)} %get-tuple-element.39), channel_id=1, source_target_pairs={{0,6},{1,7},{2,0},{3,1},{4,2},{5,3},{6,4},{7,5},{8,14},{9,15},{10,... | collective-permute-start | bytes 884744 | tf_op jit(solution)/shard_map/ppermute | solution.py:36
  324.9 51.3 %collective-permute-start.38 = (f32[1,1,9,64,128]{4,3,2,1,0:T(8,128)S(1)}, f32[1,1,9,64,128]{4,3,2,1,0:T(8,128)S(1)}, u32[]{:S(2)}, u32[]{:S(2)}) collective-permute-start(f32[1,1,9,64,128]{4,3,2,1,0:T(8,128)S(1)} %get-tuple-element.40), channel_id=1, source_target_pairs={{0,5},{1,6},{2,7},{3,0},{4,1},{5,2},{6,3},{7,4},{8,13},{9,14},{10,... | collective-permute-start | bytes 884744 | tf_op jit(solution)/shard_map/ppermute | solution.py:36
  328.2 47.2 %collective-permute-start.37 = (f32[1,1,9,64,128]{4,3,2,1,0:T(8,128)S(1)}, f32[1,1,9,64,128]{4,3,2,1,0:T(8,128)S(1)}, u32[]{:S(2)}, u32[]{:S(2)}) collective-permute-start(f32[1,1,9,64,128]{4,3,2,1,0:T(8,128)S(1)} %get-tuple-element.41), channel_id=1, source_target_pairs={{0,4},{1,5},{2,6},{3,7},{4,0},{5,1},{6,2},{7,3},{8,12},{9,13},{10,... | collective-permute-start | bytes 884744 | tf_op jit(solution)/shard_map/ppermute | solution.py:36
  469.6 26.9 %collective-permute-start.43 = (f32[4,264,4]{1,2,0:T(4,128)S(1)}, f32[4,264,4]{1,2,0:T(4,128)S(1)}, u32[]{:S(2)}, u32[]{:S(2)}) collective-permute-start(f32[4,264,4]{1,2,0:T(4,128)S(1)} %copy.37), channel_id=1, source_target_pairs={{0,1},{1,2},{2,3},{3,4},{4,5},{5,6},{6,7},{8,9},{9,10},{10,11},{11... | collective-permute-start | bytes 50696 | tf_op jit(solution)/shard_map/ppermute | solution.py:46
  473.3 23.5 %collective-permute-start.44 = (f32[4,264,4]{1,2,0:T(4,128)S(1)}, f32[4,264,4]{1,2,0:T(4,128)S(1)}, u32[]{:S(2)}, u32[]{:S(2)}) collective-permute-start(f32[4,264,4]{1,2,0:T(4,128)S(1)} %copy.38), channel_id=1, source_target_pairs={{1,0},{2,1},{3,2},{4,3},{5,4},{6,5},{7,6},{9,8},{10,9},{11,10},{12... | collective-permute-start | bytes 50696 | tf_op jit(solution)/shard_map/ppermute | solution.py:49
  564.9 9.5 collective-permute-start.59
  576.7 23.5 %collective-permute-start.61 = (f32[1,1,9,64,128]{4,3,2,1,0:T(8,128)S(1)}, f32[1,1,9,64,128]{4,3,2,1,0:T(8,128)S(1)}, u32[]{:S(2)}, u32[]{:S(2)}) collective-permute-start(f32[1,1,9,64,128]{4,3,2,1,0:T(8,128)S(1)} %get-tuple-element.35), channel_id=1, source_target_pairs={{0,3},{1,4},{2,5},{3,6},{4,7},{5,0},{6,1},{7,2},{8,11},{9,12},{10,... | collective-permute-start | bytes 884744 | tf_op jit(solution)/shard_map/ppermute | solution.py:36
  578.0 56.7 %collective-permute-start.65 = (f32[1,1,9,64,128]{4,3,2,1,0:T(8,128)S(1)}, f32[1,1,9,64,128]{4,3,2,1,0:T(8,128)S(1)}, u32[]{:S(2)}, u32[]{:S(2)}) collective-permute-start(f32[1,1,9,64,128]{4,3,2,1,0:T(8,128)S(1)} %get-tuple-element.31), channel_id=1, source_target_pairs={{0,7},{1,0},{2,1},{3,2},{4,3},{5,4},{6,5},{7,6},{8,15},{9,8},{10,9... | collective-permute-start | bytes 884744 | tf_op jit(solution)/shard_map/ppermute | solution.py:36
  580.8 53.2 %collective-permute-start.64 = (f32[1,1,9,64,128]{4,3,2,1,0:T(8,128)S(1)}, f32[1,1,9,64,128]{4,3,2,1,0:T(8,128)S(1)}, u32[]{:S(2)}, u32[]{:S(2)}) collective-permute-start(f32[1,1,9,64,128]{4,3,2,1,0:T(8,128)S(1)} %get-tuple-element.32), channel_id=1, source_target_pairs={{0,6},{1,7},{2,0},{3,1},{4,2},{5,3},{6,4},{7,5},{8,14},{9,15},{10,... | collective-permute-start | bytes 884744 | tf_op jit(solution)/shard_map/ppermute | solution.py:36
  582.0 51.3 %collective-permute-start.63 = (f32[1,1,9,64,128]{4,3,2,1,0:T(8,128)S(1)}, f32[1,1,9,64,128]{4,3,2,1,0:T(8,128)S(1)}, u32[]{:S(2)}, u32[]{:S(2)}) collective-permute-start(f32[1,1,9,64,128]{4,3,2,1,0:T(8,128)S(1)} %get-tuple-element.33), channel_id=1, source_target_pairs={{0,5},{1,6},{2,7},{3,0},{4,1},{5,2},{6,3},{7,4},{8,13},{9,14},{10,... | collective-permute-start | bytes 884744 | tf_op jit(solution)/shard_map/ppermute | solution.py:36
  585.3 47.2 %collective-permute-start.62 = (f32[1,1,9,64,128]{4,3,2,1,0:T(8,128)S(1)}, f32[1,1,9,64,128]{4,3,2,1,0:T(8,128)S(1)}, u32[]{:S(2)}, u32[]{:S(2)}) collective-permute-start(f32[1,1,9,64,128]{4,3,2,1,0:T(8,128)S(1)} %get-tuple-element.34), channel_id=1, source_target_pairs={{0,4},{1,5},{2,6},{3,7},{4,0},{5,1},{6,2},{7,3},{8,12},{9,13},{10,... | collective-permute-start | bytes 884744 | tf_op jit(solution)/shard_map/ppermute | solution.py:36
  726.7 27.2 %collective-permute-start.68 = (f32[4,264,4]{1,2,0:T(4,128)S(1)}, f32[4,264,4]{1,2,0:T(4,128)S(1)}, u32[]{:S(2)}, u32[]{:S(2)}) collective-permute-start(f32[4,264,4]{1,2,0:T(4,128)S(1)} %copy.47), channel_id=1, source_target_pairs={{0,1},{1,2},{2,3},{3,4},{4,5},{5,6},{6,7},{8,9},{9,10},{10,11},{11... | collective-permute-start | bytes 50696 | tf_op jit(solution)/shard_map/ppermute | solution.py:46
  730.4 23.8 %collective-permute-start.69 = (f32[4,264,4]{1,2,0:T(4,128)S(1)}, f32[4,264,4]{1,2,0:T(4,128)S(1)}, u32[]{:S(2)}, u32[]{:S(2)}) collective-permute-start(f32[4,264,4]{1,2,0:T(4,128)S(1)} %copy.48), channel_id=1, source_target_pairs={{1,0},{2,1},{3,2},{4,3},{5,4},{6,5},{7,6},{9,8},{10,9},{11,10},{12... | collective-permute-start | bytes 50696 | tf_op jit(solution)/shard_map/ppermute | solution.py:49
  823.0 9.5 collective-permute-start.84
  834.7 23.5 %collective-permute-start.86 = (f32[1,1,9,64,128]{4,3,2,1,0:T(8,128)S(1)}, f32[1,1,9,64,128]{4,3,2,1,0:T(8,128)S(1)}, u32[]{:S(2)}, u32[]{:S(2)}) collective-permute-start(f32[1,1,9,64,128]{4,3,2,1,0:T(8,128)S(1)} %get-tuple-element.28), channel_id=1, source_target_pairs={{0,3},{1,4},{2,5},{3,6},{4,7},{5,0},{6,1},{7,2},{8,11},{9,12},{10,... | collective-permute-start | bytes 884744 | tf_op jit(solution)/shard_map/ppermute | solution.py:36
  836.1 56.7 %collective-permute-start.90 = (f32[1,1,9,64,128]{4,3,2,1,0:T(8,128)S(1)}, f32[1,1,9,64,128]{4,3,2,1,0:T(8,128)S(1)}, u32[]{:S(2)}, u32[]{:S(2)}) collective-permute-start(f32[1,1,9,64,128]{4,3,2,1,0:T(8,128)S(1)} %get-tuple-element.24), channel_id=1, source_target_pairs={{0,7},{1,0},{2,1},{3,2},{4,3},{5,4},{6,5},{7,6},{8,15},{9,8},{10,9... | collective-permute-start | bytes 884744 | tf_op jit(solution)/shard_map/ppermute | solution.py:36
  838.8 53.2 %collective-permute-start.89 = (f32[1,1,9,64,128]{4,3,2,1,0:T(8,128)S(1)}, f32[1,1,9,64,128]{4,3,2,1,0:T(8,128)S(1)}, u32[]{:S(2)}, u32[]{:S(2)}) collective-permute-start(f32[1,1,9,64,128]{4,3,2,1,0:T(8,128)S(1)} %get-tuple-element.25), channel_id=1, source_target_pairs={{0,6},{1,7},{2,0},{3,1},{4,2},{5,3},{6,4},{7,5},{8,14},{9,15},{10,... | collective-permute-start | bytes 884744 | tf_op jit(solution)/shard_map/ppermute | solution.py:36
  840.0 51.3 %collective-permute-start.88 = (f32[1,1,9,64,128]{4,3,2,1,0:T(8,128)S(1)}, f32[1,1,9,64,128]{4,3,2,1,0:T(8,128)S(1)}, u32[]{:S(2)}, u32[]{:S(2)}) collective-permute-start(f32[1,1,9,64,128]{4,3,2,1,0:T(8,128)S(1)} %get-tuple-element.26), channel_id=1, source_target_pairs={{0,5},{1,6},{2,7},{3,0},{4,1},{5,2},{6,3},{7,4},{8,13},{9,14},{10,... | collective-permute-start | bytes 884744 | tf_op jit(solution)/shard_map/ppermute | solution.py:36
  843.4 47.2 %collective-permute-start.87 = (f32[1,1,9,64,128]{4,3,2,1,0:T(8,128)S(1)}, f32[1,1,9,64,128]{4,3,2,1,0:T(8,128)S(1)}, u32[]{:S(2)}, u32[]{:S(2)}) collective-permute-start(f32[1,1,9,64,128]{4,3,2,1,0:T(8,128)S(1)} %get-tuple-element.27), channel_id=1, source_target_pairs={{0,4},{1,5},{2,6},{3,7},{4,0},{5,1},{6,2},{7,3},{8,12},{9,13},{10,... | collective-permute-start | bytes 884744 | tf_op jit(solution)/shard_map/ppermute | solution.py:36
  984.6 27.5 %collective-permute-start.93 = (f32[4,264,4]{1,2,0:T(4,128)S(1)}, f32[4,264,4]{1,2,0:T(4,128)S(1)}, u32[]{:S(2)}, u32[]{:S(2)}) collective-permute-start(f32[4,264,4]{1,2,0:T(4,128)S(1)} %copy.57), channel_id=1, source_target_pairs={{0,1},{1,2},{2,3},{3,4},{4,5},{5,6},{6,7},{8,9},{9,10},{10,11},{11... | collective-permute-start | bytes 50696 | tf_op jit(solution)/shard_map/ppermute | solution.py:46
  988.2 24.1 %collective-permute-start.94 = (f32[4,264,4]{1,2,0:T(4,128)S(1)}, f32[4,264,4]{1,2,0:T(4,128)S(1)}, u32[]{:S(2)}, u32[]{:S(2)}) collective-permute-start(f32[4,264,4]{1,2,0:T(4,128)S(1)} %copy.58), channel_id=1, source_target_pairs={{1,0},{2,1},{3,2},{4,3},{5,4},{6,5},{7,6},{9,8},{10,9},{11,10},{12... | collective-permute-start | bytes 50696 | tf_op jit(solution)/shard_map/ppermute | solution.py:49
  (106 other events, 822.0 us)
